TPU v7x, 256 devices: a whole 4x4x8 slice. The times are simulated.
256 devices in a mesh: var: 8 (over y, core), tok: 32 (over x, z).
Axes of the slice: x: 4, y: 4, z: 8, core: 2. Of those that a mesh axis runs over, the one named last changes fastest.
Arguments:
- patches: bfloat16 [72, 4, 4096], P('var', None, 'tok'), may hold values from -6 to 6
- slot_var: int32 [72], replicated, may hold values from -1 to 47, as said below
- patch_weight: bfloat16 [48, 4, 1024], replicated, may hold values from -3 to 3
- var_embed: bfloat16 [48, 1024], replicated, may hold values from -6 to 6
- query: bfloat16 [1024], replicated, may hold values from -16 to 16
- key_weight: bfloat16 [1024, 1024], P('tok'), may hold values from -0.1875 to 0.1875
- value_weight: bfloat16 [1024, 1024], P('tok'), may hold values from -0.1875 to 0.1875
- out_weight: bfloat16 [1024, 1024], P('tok'), may hold values from -0.1875 to 0.1875
- cotangent: bfloat16 [4096, 1024], P(('tok', 'var')), may hold values from -6 to 6
Outputs:
- aggregated: bfloat16 [4096, 1024], P(('tok', 'var'))
- patch_grad: float32 [72, 4096], P('var', 'tok')
Inputs may be any that keep to these rules, and one draw needn't show every extreme that they name: `slot_var`: slot 9 * i + j belongs to index i of var. Every variable id stands in exactly one slot; empty slots hold -1. The live slots of an index come first and hold consecutive ids, rising from index to index. Every index holds at least one and at most 9 live slots, and some index holds exactly 9.
All inputs are finite; a program needn't handle non-finite values.
Results may differ from a plain program's by a relative error of at most 0.011.
Values may be sent and summed in bfloat16 or wider, within the bound.
No kernel may reach another device: no remote copies, remote signals or barrier semaphores. Data moves between devices by JAX's collectives and lax.ppermute only.
A program may use at most 128 MiB of HBM per device.

v0:
```python
import math
import jax
import jax.numpy as jnp
from jax import lax
from jax.sharding import PartitionSpec as P

H = 16
HD = 64
score_cap = 5.0
inv_sqrt_two = 1.0 / math.sqrt(2.0)
inv_sqrt_two_pi = 1.0 / math.sqrt(2.0 * math.pi)
f32 = jnp.float32
bf16 = jnp.bfloat16


def gelu_exact(inputs):
    return 0.5 * inputs * (1.0 + lax.erf(inputs * inv_sqrt_two))


def gelu_slope(inputs):
    return (
        0.5 * (1.0 + lax.erf(inputs * inv_sqrt_two))
        + inputs * jnp.exp(-0.5 * inputs * inputs) * inv_sqrt_two_pi
    )


def live_index(slot_var, var_total):
    ids = jnp.arange(var_total, dtype=jnp.int32)
    places = jnp.arange(slot_var.shape[0], dtype=jnp.int32)
    match = slot_var[None, :] == ids[:, None]
    return jnp.sum(jnp.where(match, places[None, :], 0), axis=1)


def split(x):
    hi = x.astype(bf16)
    lo = (x - hi.astype(f32)).astype(bf16)
    return (hi, lo)


def ein(spec, a, b):
    return jnp.einsum(spec, a, b, preferred_element_type=f32)


def body(
    patches,
    slot_var,
    patch_weight,
    var_embed,
    query,
    key_weight,
    value_weight,
    out_weight,
    cotangent,
    *,
    n_var,
    n_tok
):
    var_total, pixels_per, width = patch_weight.shape
    local_slots = patches.shape[0]
    rows = key_weight.shape[0]
    tok_count = cotangent.shape[0]
    query_heads = query.reshape(H, HD).astype(f32)
    wq_rows = jnp.sum(key_weight.reshape(rows, H, HD).astype(f32) * query_heads[None], axis=2)
    wq_copies = jnp.broadcast_to(wq_rows[None], (n_tok, rows, H))
    wq_full = lax.all_to_all(wq_copies, "tok", 0, 0, tiled=True).reshape(n_tok * rows, H)
    wq_hi, wq_lo = split(wq_full)
    full = lax.all_gather(jnp.stack([value_weight, out_weight]), "tok", axis=1, tiled=True)
    value_matrix = full[0]
    out_matrix = full[1]
    slot_pixels = lax.all_to_all(patches, "var", 2, 0, tiled=True)
    live_slot = live_index(slot_var, var_total)
    pixels = jnp.take(slot_pixels, live_slot, axis=0)
    pre_act = ein("vpt,vpd->vtd", pixels, patch_weight) + var_embed.astype(f32)[:, None, :]
    embedded = gelu_exact(pre_act).astype(bf16)
    raw_scores = (
        ein("vtd,dh->tvh", embedded, wq_hi) + ein("vtd,dh->tvh", embedded, wq_lo)
    ) / math.sqrt(HD)
    squashed = jnp.tanh(raw_scores / score_cap)
    exp_scores = jnp.exp(score_cap * squashed)
    attn_f32 = exp_scores / jnp.sum(exp_scores, axis=1, keepdims=True)
    attn_bf = attn_f32.astype(bf16)
    value_heads = value_matrix.reshape(width, H, HD)
    mixed_in = ein("tvh,vtd->thd", attn_bf, embedded)
    mix_hi, mix_lo = split(mixed_in)
    pooled = (
        (ein("thd,dhj->thj", mix_hi, value_heads) + ein("thd,dhj->thj", mix_lo, value_heads))
        .astype(bf16)
        .reshape(tok_count, width)
    )
    mixed_out = jnp.dot(pooled, out_matrix, preferred_element_type=f32).astype(bf16)
    contract = (((1,), (1,)), ((), ()))
    grad_pooled = (
        lax.dot_general(cotangent, out_matrix, contract, preferred_element_type=f32)
        .astype(bf16)
        .reshape(tok_count, H, HD)
    )
    spread = ein("thj,dhj->thd", grad_pooled, value_heads)
    spread_hi, spread_lo = split(spread)
    grad_attn = ein("vtd,thd->tvh", embedded, spread_hi) + ein("vtd,thd->tvh", embedded, spread_lo)
    grad_scores = attn_f32 * (grad_attn - jnp.sum(attn_f32 * grad_attn, axis=1, keepdims=True))
    grad_raw = grad_scores * (1.0 - squashed * squashed) / math.sqrt(HD)
    raw_hi, raw_lo = split(grad_raw)
    grad_embed = (
        ein("tvh,thd->vtd", attn_bf, spread_hi)
        + ein("tvh,thd->vtd", attn_bf, spread_lo)
        + ein("tvh,dh->vtd", raw_hi, wq_hi)
        + ein("tvh,dh->vtd", raw_hi, wq_lo)
        + ein("tvh,dh->vtd", raw_lo, wq_hi)
    ).astype(bf16)
    grad_pre = grad_embed.astype(f32) * gelu_slope(pre_act)
    partial = jnp.einsum(
        "vpt,vtd->vpd", pixels.astype(f32), grad_pre, precision=lax.Precision.HIGHEST
    ).reshape(var_total, pixels_per * width)
    slots = n_var * local_slots
    cols = partial.shape[1] // n_tok
    safe = jnp.clip(slot_var, 0, var_total - 1)
    slot_rows = jnp.where((slot_var >= 0)[:, None], jnp.take(partial, safe, axis=0), 0.0)
    blocks = slot_rows.reshape(n_var, local_slots, n_tok, cols).transpose(0, 2, 1, 3)
    by_var = lax.all_to_all(blocks, "var", 0, 0, tiled=True).sum(axis=0)
    by_tok = lax.all_to_all(by_var, "tok", 0, 0, tiled=True).sum(axis=0)
    del slots
    return (mixed_out, by_tok)


def solution(mesh):
    import functools

    fn = functools.partial(body, n_var=mesh.shape["var"], n_tok=mesh.shape["tok"])
    return jax.shard_map(
        fn,
        mesh=mesh,
        in_specs=(
            P("var", None, "tok"),
            P(),
            P(),
            P(),
            P(),
            P("tok", None),
            P("tok", None),
            P("tok", None),
            P(("tok", "var"), None),
        ),
        out_specs=(P(("tok", "var"), None), P("var", "tok")),
        check_vma=False,
    )
```

profile of v0, /device:TPU:32, one launch (start us, length us, event | category | flops | bytes accessed | tf_op | source)
XLA Modules:
  0.0 189.6 jit_solution(7815867198240021874)
XLA Ops:
  7.2 1.6 pad_maximum_fusion
  8.8 0.9 copy.110
  9.7 0.8 reshape.93
  10.5 4.5 %all-to-all-start.1 = ((bf16[8,2,288]{2,1,0:T(2,128)(2,1)}), bf16[8,2,288]{2,1,0:T(2,128)(2,1)S(1)}, u32[]{:S(2)}, u32[]{:S(2)}) async-start(bf16[8,2,288]{2,1,0:T(2,128)(2,1)} %reshape.93), calls=%async_computation.1 | async-start | bytes 24576 | tf_op jit(solution)/shard_map/all_to_all | solution.py:70
  15.0 1.0 reshape.72
  15.9 0.8 reshape.73
  16.9 0.8 select_reduce_fusion
  17.7 0.7 compare_and_fusion
  18.4 0.9 convert_element_type.88
  19.4 0.8 reshape.95
  20.2 0.7 broadcast_in_dim.69
  20.9 11.2 %all-to-all-start = ((f32[32,1,512]{2,1,0:T(1,128)}), f32[32,1,512]{2,1,0:T(1,128)S(1)}, u32[]{:S(2)}, u32[]{:S(2)}) async-start(f32[32,1,512]{2,1,0:T(1,128)} %reshape.95), calls=%async_computation | async-start | bytes 131072 | tf_op jit(solution)/shard_map/all_to_all | solution.py:65
  33.4 2.9 %multiply_convert_fusion = (bf16[48,16,1024]{2,1,0:T(8,128)(2,1)S(1)}, f32[48,16,1024]{2,1,0:T(8,128)}) fusion(f32[48,1024]{1,0:T(8,128)S(1)} %convert_element_type.88, bf16[48,4,1024]{2,1,0:T(4,128)(2,1)S(1)} %copy-done, bf16[48,4,16]{2,1,0:T(4,128)(2,1)S(1)} %gather_fusion, pred[48]{0:T(512)(128)(4,1)S(1)} %compare_and_fusion.1), kind=kOutput, calls=%fused_computation.17 | convolution fusion | flops 11013120 | bytes 5314608 | tf_op jit(solution)/shard_map/vpt,vpd->vtd/dot_general | solution.py:41
  36.4 5.1 %all-to-all-done = f32[32,1,512]{2,1,0:T(1,128)S(1)} async-done(((f32[32,1,512]{2,1,0:T(1,128)}), f32[32,1,512]{2,1,0:T(1,128)S(1)}, u32[]{:S(2)}, u32[]{:S(2)}) %all-to-all-start) | async-done | bytes 65568 | tf_op jit(solution)/shard_map/all_to_all | solution.py:65
  42.0 0.8 reduce
  43.1 1.0 fusion.35
  44.1 1.1 bitcast_reduce_fusion
  45.2 0.7 copy-done.14
  45.9 0.7 fusion.59
  46.6 48.1 %all-gather.2.cloned.1.call-done = bf16[2,1024,1024]{2,1,0:T(8,128)(2,1)} async-done(((bf16[2,32,1024]{2,1,0:T(8,128)(2,1)}), bf16[2,1024,1024]{2,1,0:T(8,128)(2,1)}) %all-gather.2.cloned.1.call-update) | async-done | bytes 4194320 | tf_op jit(solution)/shard_map/all_gather | solution.py:67
  94.7 3.1 %slice.12 = bf16[1,1024,1024]{2,1,0:T(8,128)(2,1)} slice(bf16[2,1024,1024]{2,1,0:T(8,128)(2,1)} %all-gather.2.cloned.1.call-done), slice={[0:1], [0:1024], [0:1024]} | slice | bytes 4194304 | tf_op jit(solution)/shard_map/slice | solution.py:68
  97.8 3.0 %copy.107 = bf16[1,1024,1024]{1,2,0:T(8,128)(2,1)S(1)} copy(bf16[1,1024,1024]{2,1,0:T(8,128)(2,1)} %slice.12) | data formatting | bytes 4194304 | tf_op jit(solution)/shard_map/slice | solution.py:68
  100.9 2.2 %fusion.28 = bf16[16,1024]{1,0:T(8,128)(2,1)S(1)} fusion(bf16[16,1024]{1,0:T(8,128)(2,1)S(1)} %copy-done.20, bf16[2,1024,1024]{2,1,0:T(8,128)(2,1)} %all-gather.2.cloned.1.call-done), kind=kOutput, calls=%fused_computation.42 | convolution fusion | flops 33570816 | bytes 2162688 | tf_op jit(solution)/shard_map/dot_general | solution.py:93
  103.1 0.8 reshape.70
  103.9 1.4 subtract_convert_fusion
  105.3 1.5 fusion.30
  106.8 2.6 %convolution_add_fusion.2 = f32[16,48,16]{1,2,0:T(8,128)S(1)} fusion(f32[16,48,16]{1,2,0:T(8,128)S(1)} %fusion.30, bf16[48,16,1024]{2,1,0:T(8,128)(2,1)S(1)} %copy-done.2, bf16[16,16,1024]{2,0,1:T(8,128)(2,1)S(1)} %get-tuple-element.8), kind=kOutput, calls=%fused_computation.37 | convolution fusion | flops 25178112 | bytes 2195456 | tf_op jit(solution)/shard_map/vtd,thd->tvh/dot_general | solution.py:41
  109.4 1.9 %subtract_convert_fusion.2 = (bf16[16,48,16]{1,2,0:T(8,128)(2,1)}, bf16[16,48,16]{1,2,0:T(8,128)(2,1)}) fusion(f32[16,48,16]{1,0,2:T(8,128)S(1)} %copy-done.15, f32[16,48,16]{1,2,0:T(8,128)S(1)} %convolution_add_fusion.2, f32[16,16]{1,0:T(8,128)S(1)} %get-tuple-element.13), kind=kOutput, calls=%fused_computation.67 | output fusion | flops 184623 | bytes 148480 | tf_op jit(solution)/shard_map/sub | solution.py:100
  111.3 1.7 copy.128
  113.0 3.3 %fusion.56 = f32[1024,16,48]{0,1,2:T(8,128)} fusion(bf16[16,48,16]{2,0,1:T(8,128)(2,1)} %copy.128, f32[1024,16]{0,1:T(8,128)} %copy-done.5), kind=kOutput, calls=%fused_computation.84 | convolution fusion | flops 25231360 | bytes 3235840 | tf_op jit(solution)/shard_map/tvh,dh->vtd/dot_general | solution.py:41
  116.4 2.3 %fusion.50 = f32[1024,16,48]{0,1,2:T(8,128)} fusion(bf16[16,48,16]{2,0,1:T(8,128)(2,1)S(1)} %copy-done.4, f32[1024,16]{0,1:T(8,128)S(1)} %copy-done.6), kind=kOutput, calls=%fused_computation.76 | convolution fusion | flops 25182208 | bytes 3235840 | tf_op jit(solution)/shard_map/tvh,dh->vtd/dot_general | solution.py:41
  118.7 2.2 %fusion.41 = f32[16,1024,48]{1,2,0:T(8,128)} fusion(bf16[16,48,16]{1,2,0:T(8,128)(2,1)S(1)} %copy-done.8, bf16[16,16,1024]{2,0,1:T(8,128)(2,1)S(1)} %get-tuple-element.8), kind=kOutput, calls=%fused_computation.57 | convolution fusion | flops 25165824 | bytes 3694592 | tf_op jit(solution)/shard_map/tvh,thd->vtd/dot_general | solution.py:41
  120.9 2.3 %fusion.44 = f32[16,1024,48]{1,2,0:T(8,128)} fusion(bf16[16,48,16]{1,2,0:T(8,128)(2,1)S(1)} %copy-done.8, bf16[16,16,1024]{2,0,1:T(8,128)(2,1)S(1)} %get-tuple-element.9), kind=kOutput, calls=%fused_computation.60 | convolution fusion | flops 25165824 | bytes 3694592 | tf_op jit(solution)/shard_map/tvh,thd->vtd/dot_general | solution.py:41
  123.4 8.5 %fusion.8 = bf16[48,16,1024]{2,1,0:T(8,128)(2,1)S(1)} fusion(f32[1024,16,48]{0,1,2:T(8,128)} %fusion.56, f32[1024,16,48]{0,1,2:T(8,128)} %fusion.50, f32[16,1024,48]{1,2,0:T(8,128)} %fusion.41, f32[16,1024,48]{1,2,0:T(8,128)} %fusion.44, bf16[16,48,16]{2,0,1:T(8,128)(2,1)S(1)} %copy.130, f32[1024,16]{0,1:T(8,128)S(1)} %copy-done.7), kind=kOutput, calls=%fused_computation.11 | convolution fusion | flops 29114368 | bytes 14245888 | tf_op jit(solution)/shard_map/tvh,dh->vtd/dot_general | solution.py:41
  131.9 3.2 %fusion.6 = f32[48,4,1024]{2,1,0:T(4,128)S(1)} fusion(bf16[48,16,1024]{2,1,0:T(8,128)(2,1)S(1)} %fusion.8, f32[48,16,1024]{2,1,0:T(8,128)S(1)} %copy-done.3, f32[48,1024]{1,0:T(8,128)S(1)} %copy-done.11, bf16[48,4,16]{2,1,0:T(4,128)(2,1)S(1)} %copy-done.13, pred[48]{0:T(512)(128)(4,1)S(1)} %copy-done.19), kind=kOutput, calls=%fused_computation.9 | convolution fusion | flops 46402560 | bytes 5707824 | tf_op jit(solution)/shard_map/vpt,vtd->vpd/dot_general | solution.py:111
  135.6 2.0 %gather_fusion.1 = f32[72,4096]{1,0:T(8,128)} fusion(f32[48,4096]{1,0:T(8,128)S(1)} %bitcast.98, s32[1024]{0:T(1024)S(1)} %pad_clamp_fusion), kind=kCustom, calls=%fused_computation.1 | custom fusion | bytes 2359584 | tf_op jit(solution)/shard_map/jit(_take)/gather | solution.py:117
  137.6 1.5 copy.134
  139.1 1.3 select_bitcast_fusion
  140.4 4.3 %all-to-all-start.2 = ((f32[8,32,9,128]{3,1,2,0:T(8,128)}), f32[8,32,9,128]{3,1,2,0:T(8,128)}, u32[]{:S(2)}, u32[]{:S(2)}) async-start(f32[8,32,9,128]{3,1,2,0:T(8,128)} %select_bitcast_fusion), calls=%async_computation.2 | async-start | bytes 2359296 | tf_op jit(solution)/shard_map/all_to_all | solution.py:119
  144.7 3.2 %subtract_convert_fusion.1 = (bf16[16,16,1024]{2,1,0:T(8,128)(2,1)S(1)}, bf16[16,16,1024]{2,1,0:T(8,128)(2,1)S(1)}) fusion(bf16[16,48,16]{1,2,0:T(8,128)(2,1)S(1)} %copy-done.9, bf16[48,16,1024]{2,1,0:T(8,128)(2,1)} %copy-done.1), kind=kOutput, calls=%fused_computation.44 | convolution fusion | flops 26214400 | bytes 2646016 | tf_op jit(solution)/shard_map/tvh,vtd->thd/dot_general | solution.py:41
  147.9 0.6 fusion.38
  148.5 13.6 %all-to-all-done.2 = f32[8,32,9,128]{3,1,2,0:T(8,128)} async-done(((f32[8,32,9,128]{3,1,2,0:T(8,128)}), f32[8,32,9,128]{3,1,2,0:T(8,128)}, u32[]{:S(2)}, u32[]{:S(2)}) %all-to-all-start.2) | async-done | bytes 1179680 | tf_op jit(solution)/shard_map/all_to_all | solution.py:119
  162.1 1.4 reduce_sum.61
  163.5 0.8 copy.131
  164.3 5.8 %all-to-all-start.3 = ((f32[32,9,128]{2,1,0:T(8,128)}), f32[32,9,128]{2,1,0:T(8,128)S(1)}, u32[]{:S(2)}, u32[]{:S(2)}) async-start(f32[32,9,128]{2,1,0:T(8,128)} %copy.131), calls=%async_computation.3 | async-start | bytes 524288 | tf_op jit(solution)/shard_map/all_to_all | solution.py:120
  170.1 0.7 fusion.25
  170.9 2.6 %fusion.26 = bf16[16,1024]{1,0:T(8,128)(2,1)} fusion(bf16[16,1024]{1,0:T(8,128)(2,1)S(1)} %reshape.69, bf16[2,1024,1024]{2,1,0:T(8,128)(2,1)} %all-gather.2.cloned.1.call-done), kind=kOutput, calls=%fused_computation.40 | convolution fusion | flops 33570816 | bytes 2162688 | tf_op jit(solution)/shard_map/dot_general | solution.py:90
  173.5 8.6 %all-to-all-done.3 = f32[32,9,128]{2,1,0:T(8,128)S(1)} async-done(((f32[32,9,128]{2,1,0:T(8,128)}), f32[32,9,128]{2,1,0:T(8,128)S(1)}, u32[]{:S(2)}, u32[]{:S(2)}) %all-to-all-start.3) | async-done | bytes 147488 | tf_op jit(solution)/shard_map/all_to_all | solution.py:120
  (65 shorter events, 4.2 us)
Async XLA Ops:
  7.2 26.2 %copy-start = (bf16[48,4,1024]{2,1,0:T(4,128)(2,1)S(1)}, bf16[48,4,1024]{2,1,0:T(4,128)(2,1)}, u32[]{:S(2)}) copy-start(bf16[48,4,1024]{2,1,0:T(4,128)(2,1)} %param.11) | copy-start | bytes 1179652
  7.2 87.5 %all-gather.2.cloned.1.call-start = ((), (), s32[]{:S(2)}) async-start(), calls=%async_computation.4 | async-start | bytes 4325376 | tf_op jit(solution)/shard_map/all_gather | solution.py:67
  10.5 10.4 %all-to-all-start.1 = ((bf16[8,2,288]{2,1,0:T(2,128)(2,1)}), bf16[8,2,288]{2,1,0:T(2,128)(2,1)S(1)}, u32[]{:S(2)}, u32[]{:S(2)}) async-start(bf16[8,2,288]{2,1,0:T(2,128)(2,1)} %reshape.93), calls=%async_computation.1 | async-start | bytes 24576 | tf_op jit(solution)/shard_map/all_to_all | solution.py:70
  17.7 18.6 %copy-start.18 = (pred[48]{0:T(512)(128)(4,1)}, pred[48]{0:T(512)(128)(4,1)S(1)}, u32[]{:S(2)}) copy-start(pred[48]{0:T(512)(128)(4,1)S(1)} %compare_and_fusion.1) | copy-start | bytes 148
  19.3 17.0 %copy-start.10 = (f32[48,1024]{1,0:T(8,128)}, f32[48,1024]{1,0:T(8,128)S(1)}, u32[]{:S(2)}) copy-start(f32[48,1024]{1,0:T(8,128)S(1)} %convert_element_type.88) | copy-start | bytes 589828
  20.9 20.6 %all-to-all-start = ((f32[32,1,512]{2,1,0:T(1,128)}), f32[32,1,512]{2,1,0:T(1,128)S(1)}, u32[]{:S(2)}, u32[]{:S(2)}) async-start(f32[32,1,512]{2,1,0:T(1,128)} %reshape.95), calls=%async_computation | async-start | bytes 131072 | tf_op jit(solution)/shard_map/all_to_all | solution.py:65
  33.4 8.0 %copy-start.12 = (bf16[48,4,16]{2,1,0:T(4,128)(2,1)}, bf16[48,4,16]{2,1,0:T(4,128)(2,1)S(1)}, u32[]{:S(2)}) copy-start(bf16[48,4,16]{2,1,0:T(4,128)(2,1)S(1)} %gather_fusion) | copy-start | bytes 18436
  36.4 58.3 %copy-start.1 = (bf16[48,16,1024]{2,1,0:T(8,128)(2,1)}, bf16[48,16,1024]{2,1,0:T(8,128)(2,1)S(1)}, u32[]{:S(2)}) copy-start(bf16[48,16,1024]{2,1,0:T(8,128)(2,1)S(1)} %get-tuple-element.11) | copy-start | bytes 4718596
  43.1 51.6 %copy-start.5 = (f32[1024,16]{0,1:T(8,128)}, f32[1024,16]{0,1:T(8,128)S(1)}, u32[]{:S(2)}) copy-start(f32[1024,16]{0,1:T(8,128)S(1)} %reshape.68) | copy-start | bytes 196612
  45.2 0.7 copy-start.14
  46.6 54.3 %copy-start.20 = (bf16[16,1024]{1,0:T(8,128)(2,1)S(1)}, bf16[16,1024]{1,0:T(8,128)(2,1)}, u32[]{:S(2)}) copy-start(bf16[16,1024]{1,0:T(8,128)(2,1)} %param.17) | copy-start | bytes 98308
  103.9 1.4 copy-start.2
  105.2 4.2 %copy-start.15 = (f32[16,48,16]{1,0,2:T(8,128)S(1)}, f32[16,48,16]{1,0,2:T(8,128)}, u32[]{:S(2)}) copy-start(f32[16,48,16]{1,0,2:T(8,128)} %copy-done.14) | copy-start | bytes 147460
  113.0 3.3 %copy-start.4 = (bf16[16,48,16]{2,0,1:T(8,128)(2,1)S(1)}, bf16[16,48,16]{2,0,1:T(8,128)(2,1)}, u32[]{:S(2)}) copy-start(bf16[16,48,16]{2,0,1:T(8,128)(2,1)} %copy.128) | copy-start | bytes 73732
  113.0 3.3 %copy-start.6 = (f32[1024,16]{0,1:T(8,128)S(1)}, f32[1024,16]{0,1:T(8,128)}, u32[]{:S(2)}) copy-start(f32[1024,16]{0,1:T(8,128)} %copy-done.5) | copy-start | bytes 196612
  113.0 5.6 %copy-start.8 = (bf16[16,48,16]{1,2,0:T(8,128)(2,1)S(1)}, bf16[16,48,16]{1,2,0:T(8,128)(2,1)}, u32[]{:S(2)}) copy-start(bf16[16,48,16]{1,2,0:T(8,128)(2,1)} %fusion.59) | copy-start | bytes 73732
  120.9 2.3 %copy-start.16 = (bf16[16,48,16]{1,2,0:T(8,128)(2,1)S(1)}, bf16[16,48,16]{1,2,0:T(8,128)(2,1)}, u32[]{:S(2)}) copy-start(bf16[16,48,16]{1,2,0:T(8,128)(2,1)} %get-tuple-element.4) | copy-start | bytes 73732
  120.9 2.5 %copy-start.7 = (f32[1024,16]{0,1:T(8,128)S(1)}, f32[1024,16]{0,1:T(8,128)}, u32[]{:S(2)}) copy-start(f32[1024,16]{0,1:T(8,128)} %copy-done.5) | copy-start | bytes 196612
  123.4 8.5 %copy-start.3 = (f32[48,16,1024]{2,1,0:T(8,128)S(1)}, f32[48,16,1024]{2,1,0:T(8,128)}, u32[]{:S(2)}) copy-start(f32[48,16,1024]{2,1,0:T(8,128)} %get-tuple-element.12) | copy-start | bytes 9437188
  123.4 8.5 %copy-start.11 = (f32[48,1024]{1,0:T(8,128)S(1)}, f32[48,1024]{1,0:T(8,128)}, u32[]{:S(2)}) copy-start(f32[48,1024]{1,0:T(8,128)} %copy-done.10) | copy-start | bytes 589828
  123.4 8.5 %copy-start.13 = (bf16[48,4,16]{2,1,0:T(4,128)(2,1)S(1)}, bf16[48,4,16]{2,1,0:T(4,128)(2,1)}, u32[]{:S(2)}) copy-start(bf16[48,4,16]{2,1,0:T(4,128)(2,1)} %copy-done.12) | copy-start | bytes 18436
  123.4 8.5 %copy-start.19 = (pred[48]{0:T(512)(128)(4,1)S(1)}, pred[48]{0:T(512)(128)(4,1)}, u32[]{:S(2)}) copy-start(pred[48]{0:T(512)(128)(4,1)} %copy-done.18) | copy-start | bytes 148
  135.6 3.5 %copy-start.17 = (pred[8,9]{1,0:T(8,128)(4,1)S(1)}, pred[8,9]{1,0:T(8,128)(4,1)}, u32[]{:S(2)}) copy-start(pred[8,9]{1,0:T(8,128)(4,1)} %broadcast_in_dim.69) | copy-start | bytes 220
  137.6 7.1 %copy-start.9 = (bf16[16,48,16]{1,2,0:T(8,128)(2,1)S(1)}, bf16[16,48,16]{1,2,0:T(8,128)(2,1)}, u32[]{:S(2)}) copy-start(bf16[16,48,16]{1,2,0:T(8,128)(2,1)} %fusion.59) | copy-start | bytes 73732
  140.4 21.7 %all-to-all-start.2 = ((f32[8,32,9,128]{3,1,2,0:T(8,128)}), f32[8,32,9,128]{3,1,2,0:T(8,128)}, u32[]{:S(2)}, u32[]{:S(2)}) async-start(f32[8,32,9,128]{3,1,2,0:T(8,128)} %select_bitcast_fusion), calls=%async_computation.2 | async-start | bytes 2359296 | tf_op jit(solution)/shard_map/all_to_all | solution.py:119
  164.3 17.8 %all-to-all-start.3 = ((f32[32,9,128]{2,1,0:T(8,128)}), f32[32,9,128]{2,1,0:T(8,128)S(1)}, u32[]{:S(2)}, u32[]{:S(2)}) async-start(f32[32,9,128]{2,1,0:T(8,128)} %copy.131), calls=%async_computation.3 | async-start | bytes 524288 | tf_op jit(solution)/shard_map/all_to_all | solution.py:120
Sparse Core Ops, SparseCore 0:
  10.6 84.0 all-gather.1
where the time goes:
time: 190 us
  waiting for transfers between devices  75.3 us (40%)
  matrix products  41.6 us (22%)
  starting transfers between devices  25.8 us (14%)
  local copies, waits for them, and re-layouts  21.7 us (11%)
  between operations  14.4 us (8%)
  other arithmetic  10.8 us (6%)
    all_gather x1, waiting for transfers between devices, body(): lax.all_gather(jnp.stack([value_weight, out_weight]), 'tok', axis=1, tile...  48.1 us
    dot_general x14, matrix products, ein(): return jnp.einsum(spec, a, b, preferred_element_type=f32)  33.6 us
    all_to_all x1, waiting for transfers between devices, body(): by_var = lax.all_to_all(blocks, 'var', 0, 0, tiled=True).sum(axis=0)  13.6 us
    all_to_all x1, starting transfers between devices, body(): lax.all_to_all(wq_copies, 'tok', 0, 0, tiled=True).reshape(n_tok * rows, H)  11.2 us
    all_to_all x1, waiting for transfers between devices, body(): by_tok = lax.all_to_all(by_var, 'tok', 0, 0, tiled=True).sum(axis=0)  8.57 us
    slice x2, local copies, waits for them, and re-layouts, body(): value_matrix = full[0]  6.18 us
    all_to_all x1, starting transfers between devices, body(): by_tok = lax.all_to_all(by_var, 'tok', 0, 0, tiled=True).sum(axis=0)  5.8 us
    unnamed x50, local copies, waits for them, and re-layouts  5.65 us
  transfers between devices with their start and end apart: 5, of which 4 were waited for; matrix products, arithmetic and copies ran while one was open for 12% of the time, Pallas kernels for 0%

commit v1 on v0

--- a/solution.py
+++ b/solution.py
@@ -64,7 +64,11 @@
     wq_copies = jnp.broadcast_to(wq_rows[None], (n_tok, rows, H))
     wq_full = lax.all_to_all(wq_copies, "tok", 0, 0, tiled=True).reshape(n_tok * rows, H)
     wq_hi, wq_lo = split(wq_full)
-    full = lax.all_gather(jnp.stack([value_weight, out_weight]), "tok", axis=1, tiled=True)
+    value = jnp.stack([value_weight, out_weight])
+    size = lax.axis_size("tok")
+    tiles = jnp.stack([value for _ in range(size)])
+    tiles = lax.all_to_all(tiles, "tok", split_axis=0, concat_axis=0)
+    full = jnp.concatenate(tiles, axis=1)
     value_matrix = full[0]
     out_matrix = full[1]
     slot_pixels = lax.all_to_all(patches, "var", 2, 0, tiled=True)

time: 190 us -> 231 us (1.22)
  waiting for transfers between devices: 75.3 us -> 117 us
  between operations: 14.4 us -> 1.05 us
  local copies, waits for them, and re-layouts: 21.7 us -> 31.1 us
  starting transfers between devices: 25.8 us -> 31.8 us
  other arithmetic: 10.8 us -> 7.87 us
    all_to_all x0 -> x1, waiting for transfers between devices: none -> 83.9 us  [body(): tiles = lax.all_to_all(tiles, 'tok', split_axis=0, concat_axis=0)]
    all_gather x1 -> x0, waiting for transfers between devices: 48.1 us -> none  [body(): lax.all_gather(jnp.stack([value_weight, out_weight]), 'tok', axis=1, tile...]
    another operation x0 -> x3, local copies, waits for them, and re-layouts: none -> 11.1 us  [the longest x2 8.61 us: body(): value_heads = value_matrix.reshape(width, H, HD)]
    all_to_all x0 -> x1, starting transfers between devices: none -> 5.73 us  [body(): tiles = lax.all_to_all(tiles, 'tok', split_axis=0, concat_axis=0)]
    slice x2 -> x1, local copies, waits for them, and re-layouts: 6.18 us -> 1.8 us  [body(): out_matrix = full[1]]
    all_to_all x1, waiting for transfers between devices: 5.08 us -> 8.21 us  [body(): lax.all_to_all(wq_copies, 'tok', 0, 0, tiled=True).reshape(n_tok * rows, H)]
    all_to_all x0 -> x1, local copies, waits for them, and re-layouts: none -> 2.63 us  [body(): tiles = lax.all_to_all(tiles, 'tok', split_axis=0, concat_axis=0)]
    all_to_all x1, waiting for transfers between devices: 0.01 us -> 2.57 us  [body(): slot_pixels = lax.all_to_all(patches, 'var', 2, 0, tiled=True)]
  transfers between devices with their start and end apart: 5 -> 5, of which waited for: 4 -> 5; matrix products, arithmetic and copies ran while one was open for 12% -> 9% of each run, Pallas kernels for 0% -> 0%
where the time goes in v1:
time: 231 us; the launch traced here: 230 us
  waiting for transfers between devices  117 us (51%)
  matrix products  41.5 us (18%)
  starting transfers between devices  31.8 us (14%)
  local copies, waits for them, and re-layouts  31.1 us (13%)
  other arithmetic  7.87 us (3%)
    all_to_all x1, waiting for transfers between devices, body(): tiles = lax.all_to_all(tiles, 'tok', split_axis=0, concat_axis=0)  83.9 us
    dot_general x14, matrix products, ein(): return jnp.einsum(spec, a, b, preferred_element_type=f32)  33.5 us
    all_to_all x1, waiting for transfers between devices, body(): by_var = lax.all_to_all(blocks, 'var', 0, 0, tiled=True).sum(axis=0)  13.5 us
    all_to_all x1, starting transfers between devices, body(): lax.all_to_all(wq_copies, 'tok', 0, 0, tiled=True).reshape(n_tok * rows, H)  11.2 us
    another operation x2, local copies, waits for them, and re-layouts, body(): value_heads = value_matrix.reshape(width, H, HD)  8.61 us
    all_to_all x1, waiting for transfers between devices, body(): by_tok = lax.all_to_all(by_var, 'tok', 0, 0, tiled=True).sum(axis=0)  8.58 us
    all_to_all x1, waiting for transfers between devices, body(): lax.all_to_all(wq_copies, 'tok', 0, 0, tiled=True).reshape(n_tok * rows, H)  8.21 us
    all_to_all x1, starting transfers between devices, body(): by_tok = lax.all_to_all(by_var, 'tok', 0, 0, tiled=True).sum(axis=0)  6.12 us
  transfers between devices with their start and end apart: 5, of which 5 were waited for; matrix products, arithmetic and copies ran while one was open for 9% of the time, Pallas kernels for 0%

profile of v1, /device:TPU:32, one launch (start us, length us, event | category | flops | bytes accessed | tf_op | source)
XLA Modules:
  0.0 230.1 jit_solution(16088340792761794618)
XLA Ops:
  0.6 0.9 copy.120
  1.6 0.8 reshape.104
  2.4 4.5 %all-to-all-start.2 = ((bf16[8,2,288]{2,1,0:T(2,128)(2,1)}), bf16[8,2,288]{2,1,0:T(2,128)(2,1)S(1)}, u32[]{:S(2)}, u32[]{:S(2)}) async-start(bf16[8,2,288]{2,1,0:T(2,128)(2,1)} %reshape.104), calls=%async_computation.2 | async-start | bytes 24576 | tf_op jit(solution)/shard_map/all_to_all | solution.py:74
  6.8 1.0 reshape.83
  7.8 0.8 reshape.84
  8.8 0.8 reshape.106
  9.6 2.6 %all-to-all-done.2 = bf16[8,2,288]{2,1,0:T(2,128)(2,1)S(1)} async-done(((bf16[8,2,288]{2,1,0:T(2,128)(2,1)}), bf16[8,2,288]{2,1,0:T(2,128)(2,1)S(1)}, u32[]{:S(2)}, u32[]{:S(2)}) %all-to-all-start.2) | async-done | bytes 9248 | tf_op jit(solution)/shard_map/all_to_all | solution.py:74
  12.2 11.2 %all-to-all-start.1 = ((f32[32,1,512]{2,1,0:T(1,128)}), f32[32,1,512]{2,1,0:T(1,128)S(1)}, u32[]{:S(2)}, u32[]{:S(2)}) async-start(f32[32,1,512]{2,1,0:T(1,128)} %reshape.106), calls=%async_computation.1 | async-start | bytes 131072 | tf_op jit(solution)/shard_map/all_to_all | solution.py:65
  23.4 0.9 pad_maximum_fusion
  24.2 8.2 %all-to-all-done.1 = f32[32,1,512]{2,1,0:T(1,128)S(1)} async-done(((f32[32,1,512]{2,1,0:T(1,128)}), f32[32,1,512]{2,1,0:T(1,128)S(1)}, u32[]{:S(2)}, u32[]{:S(2)}) %all-to-all-start.1) | async-done | bytes 65568 | tf_op jit(solution)/shard_map/all_to_all | solution.py:65
  32.5 2.5 %stack.11 = bf16[32,2,32,1024]{3,2,1,0:T(8,128)(2,1)} broadcast(bf16[2,32,1024]{2,1,0:T(8,128)(2,1)S(1)} %pad_maximum_fusion), dimensions={1,2,3} | broadcast | bytes 4325376 | tf_op jit(solution)/shard_map/stack | solution.py:69
  35.0 5.7 %all-to-all-start = ((bf16[32,2,32,1024]{3,2,1,0:T(8,128)(2,1)}), bf16[32,2,32,1024]{3,2,1,0:T(8,128)(2,1)}, u32[]{:S(2)}, u32[]{:S(2)}) async-start(bf16[32,2,32,1024]{3,2,1,0:T(8,128)(2,1)} %stack.11), calls=%async_computation | async-start | bytes 8388608 | tf_op jit(solution)/shard_map/all_to_all | solution.py:70
  40.9 0.7 broadcast_in_dim.69
  43.0 2.9 %multiply_convert_fusion = (bf16[48,16,1024]{2,1,0:T(8,128)(2,1)S(1)}, f32[48,16,1024]{2,1,0:T(8,128)}) fusion(f32[48,1024]{1,0:T(8,128)S(1)} %convert_element_type.88, bf16[48,4,1024]{2,1,0:T(4,128)(2,1)S(1)} %copy-done, bf16[48,4,16]{2,1,0:T(4,128)(2,1)S(1)} %gather_fusion, pred[48]{0:T(512)(128)(4,1)S(1)} %compare_and_fusion.1), kind=kOutput, calls=%fused_computation.18 | convolution fusion | flops 11013120 | bytes 5314608 | tf_op jit(solution)/shard_map/vpt,vpd->vtd/dot_general | solution.py:41
  46.5 0.8 reduce
  47.7 1.0 fusion.31
  48.6 1.1 bitcast_reduce_fusion
  50.4 0.7 fusion.55
  51.2 83.9 %all-to-all-done = bf16[32,2,32,1024]{3,2,1,0:T(8,128)(2,1)} async-done(((bf16[32,2,32,1024]{3,2,1,0:T(8,128)(2,1)}), bf16[32,2,32,1024]{3,2,1,0:T(8,128)(2,1)}, u32[]{:S(2)}, u32[]{:S(2)}) %all-to-all-start) | async-done | bytes 4194336 | tf_op jit(solution)/shard_map/all_to_all | solution.py:70
  135.1 2.6 %copy.184 = bf16[32,2,32,1024]{3,2,0,1:T(8,128)(2,1)S(1)} copy(bf16[32,2,32,1024]{3,2,1,0:T(8,128)(2,1)} %all-to-all-done) | data formatting | bytes 8388608 | tf_op jit(solution)/shard_map/all_to_all | solution.py:70
  137.8 1.8 fusion.62
  139.6 4.0 %reshape_squeeze.3 = bf16[1024,16,64]{2,1,0:T(8,128)(2,1)} reshape(bf16[1,32,32,1024]{3,2,1,0:T(8,128)(2,1)S(1)} %get-tuple-element.9) | data formatting | bytes 4194304 | tf_op jit(solution)/shard_map/reshape;squeeze | solution.py:86
  143.5 4.6 %copy.126 = bf16[1024,16,64]{0,2,1:T(8,128)(2,1)S(1)} copy(bf16[1024,16,64]{2,1,0:T(8,128)(2,1)} %reshape_squeeze.3) | data formatting | bytes 4194304 | tf_op jit(solution)/shard_map/reshape;squeeze | solution.py:86
  148.2 2.2 fusion.24
  150.4 0.7 reshape.81
  151.2 1.4 subtract_convert_fusion
  152.6 1.5 fusion.26
  154.1 2.6 %convolution_add_fusion.2 = f32[16,48,16]{1,2,0:T(8,128)S(1)} fusion(f32[16,48,16]{1,2,0:T(8,128)S(1)} %fusion.26, bf16[48,16,1024]{2,1,0:T(8,128)(2,1)S(1)} %copy-done.2, bf16[16,16,1024]{2,0,1:T(8,128)(2,1)S(1)} %get-tuple-element.10), kind=kOutput, calls=%fused_computation.35 | convolution fusion | flops 25178112 | bytes 2195456 | tf_op jit(solution)/shard_map/vtd,thd->tvh/dot_general | solution.py:41
  156.7 1.9 subtract_convert_fusion.2
  158.6 1.7 copy.141
  160.3 3.2 %fusion.52 = f32[1024,16,48]{0,1,2:T(8,128)} fusion(bf16[16,48,16]{2,0,1:T(8,128)(2,1)} %copy.141, f32[1024,16]{0,1:T(8,128)} %copy-done.5), kind=kOutput, calls=%fused_computation.82 | convolution fusion | flops 25231360 | bytes 3235840 | tf_op jit(solution)/shard_map/tvh,dh->vtd/dot_general | solution.py:41
  163.6 2.2 fusion.46
  165.8 2.4 %fusion.37 = f32[16,1024,48]{1,2,0:T(8,128)} fusion(bf16[16,48,16]{1,2,0:T(8,128)(2,1)S(1)} %copy-done.8, bf16[16,16,1024]{2,0,1:T(8,128)(2,1)S(1)} %get-tuple-element.10), kind=kOutput, calls=%fused_computation.55 | convolution fusion | flops 25165824 | bytes 3694592 | tf_op jit(solution)/shard_map/tvh,thd->vtd/dot_general | solution.py:41
  168.2 2.3 fusion.40
  170.7 8.5 %fusion.8 = bf16[48,16,1024]{2,1,0:T(8,128)(2,1)S(1)} fusion(f32[1024,16,48]{0,1,2:T(8,128)} %fusion.52, f32[1024,16,48]{0,1,2:T(8,128)} %fusion.46, f32[16,1024,48]{1,2,0:T(8,128)} %fusion.37, f32[16,1024,48]{1,2,0:T(8,128)} %fusion.40, bf16[16,48,16]{2,0,1:T(8,128)(2,1)S(1)} %copy.143, f32[1024,16]{0,1:T(8,128)S(1)} %copy-done.7), kind=kOutput, calls=%fused_computation.12 | convolution fusion | flops 29114368 | bytes 14245888 | tf_op jit(solution)/shard_map/tvh,dh->vtd/dot_general | solution.py:41
  179.2 3.2 %fusion.6 = f32[48,4,1024]{2,1,0:T(4,128)S(1)} fusion(bf16[48,16,1024]{2,1,0:T(8,128)(2,1)S(1)} %fusion.8, f32[48,16,1024]{2,1,0:T(8,128)S(1)} %copy-done.3, f32[48,1024]{1,0:T(8,128)S(1)} %copy-done.11, bf16[48,4,16]{2,1,0:T(4,128)(2,1)S(1)} %copy-done.13, pred[48]{0:T(512)(128)(4,1)S(1)} %copy-done.21), kind=kOutput, calls=%fused_computation.10 | convolution fusion | flops 46402560 | bytes 5707824 | tf_op jit(solution)/shard_map/vpt,vtd->vpd/dot_general | solution.py:115
  182.9 2.0 gather_fusion.1
  184.8 1.5 copy.147
  186.4 1.2 select_bitcast_fusion
  187.6 4.3 %all-to-all-start.3 = ((f32[8,32,9,128]{3,1,2,0:T(8,128)}), f32[8,32,9,128]{3,1,2,0:T(8,128)}, u32[]{:S(2)}, u32[]{:S(2)}) async-start(f32[8,32,9,128]{3,1,2,0:T(8,128)} %select_bitcast_fusion), calls=%async_computation.3 | async-start | bytes 2359296 | tf_op jit(solution)/shard_map/all_to_all | solution.py:123
  191.8 3.2 %subtract_convert_fusion.1 = (bf16[16,16,1024]{2,1,0:T(8,128)(2,1)S(1)}, bf16[16,16,1024]{2,1,0:T(8,128)(2,1)S(1)}) fusion(bf16[16,48,16]{1,2,0:T(8,128)(2,1)S(1)} %copy-done.9, bf16[48,16,1024]{2,1,0:T(8,128)(2,1)} %copy-done.1), kind=kOutput, calls=%fused_computation.42 | convolution fusion | flops 26214400 | bytes 2646016 | tf_op jit(solution)/shard_map/tvh,vtd->thd/dot_general | solution.py:41
  195.7 13.5 %all-to-all-done.3 = f32[8,32,9,128]{3,1,2,0:T(8,128)} async-done(((f32[8,32,9,128]{3,1,2,0:T(8,128)}), f32[8,32,9,128]{3,1,2,0:T(8,128)}, u32[]{:S(2)}, u32[]{:S(2)}) %all-to-all-start.3) | async-done | bytes 1179680 | tf_op jit(solution)/shard_map/all_to_all | solution.py:123
  209.2 1.4 reduce_sum.61
  210.5 0.8 copy.144
  211.3 6.1 %all-to-all-start.4 = ((f32[32,9,128]{2,1,0:T(8,128)}), f32[32,9,128]{2,1,0:T(8,128)S(1)}, u32[]{:S(2)}, u32[]{:S(2)}) async-start(f32[32,9,128]{2,1,0:T(8,128)} %copy.144), calls=%async_computation.4 | async-start | bytes 524288 | tf_op jit(solution)/shard_map/all_to_all | solution.py:124
  217.5 0.7 fusion.23
  218.3 2.6 %convolution_convert_fusion.1 = bf16[16,1024]{1,0:T(8,128)(2,1)} fusion(bf16[16,1024]{1,0:T(8,128)(2,1)S(1)} %reshape.80, bf16[1024,1024]{1,0:T(8,128)(2,1)} %bitcast.97), kind=kOutput, calls=%fused_computation.39 | convolution fusion | flops 33570816 | bytes 2162688 | tf_op jit(solution)/shard_map/dot_general | solution.py:94
  220.9 8.6 %all-to-all-done.4 = f32[32,9,128]{2,1,0:T(8,128)S(1)} async-done(((f32[32,9,128]{2,1,0:T(8,128)}), f32[32,9,128]{2,1,0:T(8,128)S(1)}, u32[]{:S(2)}, u32[]{:S(2)}) %all-to-all-start.4) | async-done | bytes 147488 | tf_op jit(solution)/shard_map/all_to_all | solution.py:124
  (71 shorter events, 5.6 us)
Async XLA Ops:
  0.6 42.4 %copy-start = (bf16[48,4,1024]{2,1,0:T(4,128)(2,1)S(1)}, bf16[48,4,1024]{2,1,0:T(4,128)(2,1)}, u32[]{:S(2)}) copy-start(bf16[48,4,1024]{2,1,0:T(4,128)(2,1)} %param.11) | copy-start | bytes 1179652
  2.4 9.8 %all-to-all-start.2 = ((bf16[8,2,288]{2,1,0:T(2,128)(2,1)}), bf16[8,2,288]{2,1,0:T(2,128)(2,1)S(1)}, u32[]{:S(2)}, u32[]{:S(2)}) async-start(bf16[8,2,288]{2,1,0:T(2,128)(2,1)} %reshape.104), calls=%async_computation.2 | async-start | bytes 24576 | tf_op jit(solution)/shard_map/all_to_all | solution.py:74
  12.2 20.3 %all-to-all-start.1 = ((f32[32,1,512]{2,1,0:T(1,128)}), f32[32,1,512]{2,1,0:T(1,128)S(1)}, u32[]{:S(2)}, u32[]{:S(2)}) async-start(f32[32,1,512]{2,1,0:T(1,128)} %reshape.106), calls=%async_computation.1 | async-start | bytes 131072 | tf_op jit(solution)/shard_map/all_to_all | solution.py:65
  35.0 5.7 %copy-start.16 = (bf16[48,1024]{1,0:T(8,128)(2,1)S(1)}, bf16[48,1024]{1,0:T(8,128)(2,1)}, u32[]{:S(2)}) copy-start(bf16[48,1024]{1,0:T(8,128)(2,1)} %param.12) | copy-start | bytes 294916
  35.0 5.8 %copy-start.22 = (s32[72]{0:T(128)S(1)}, s32[72]{0:T(128)}, u32[]{:S(2)}) copy-start(s32[72]{0:T(128)} %param.10) | copy-start | bytes 868
  35.0 100.1 %all-to-all-start = ((bf16[32,2,32,1024]{3,2,1,0:T(8,128)(2,1)}), bf16[32,2,32,1024]{3,2,1,0:T(8,128)(2,1)}, u32[]{:S(2)}, u32[]{:S(2)}) async-start(bf16[32,2,32,1024]{3,2,1,0:T(8,128)(2,1)} %stack.11), calls=%async_computation | async-start | bytes 8388608 | tf_op jit(solution)/shard_map/all_to_all | solution.py:70
  40.8 5.8 %copy-start.10 = (f32[48,1024]{1,0:T(8,128)}, f32[48,1024]{1,0:T(8,128)S(1)}, u32[]{:S(2)}) copy-start(f32[48,1024]{1,0:T(8,128)S(1)} %convert_element_type.88) | copy-start | bytes 589828
  41.7 4.3 %copy-start.20 = (pred[48]{0:T(512)(128)(4,1)}, pred[48]{0:T(512)(128)(4,1)S(1)}, u32[]{:S(2)}) copy-start(pred[48]{0:T(512)(128)(4,1)S(1)} %compare_and_fusion.1) | copy-start | bytes 148
  43.0 2.9 %copy-start.12 = (bf16[48,4,16]{2,1,0:T(4,128)(2,1)}, bf16[48,4,16]{2,1,0:T(4,128)(2,1)S(1)}, u32[]{:S(2)}) copy-start(bf16[48,4,16]{2,1,0:T(4,128)(2,1)S(1)} %gather_fusion) | copy-start | bytes 18436
  46.0 91.8 %copy-start.1 = (bf16[48,16,1024]{2,1,0:T(8,128)(2,1)}, bf16[48,16,1024]{2,1,0:T(8,128)(2,1)S(1)}, u32[]{:S(2)}) copy-start(bf16[48,16,1024]{2,1,0:T(8,128)(2,1)S(1)} %get-tuple-element.13) | copy-start | bytes 4718596
  47.7 90.1 %copy-start.5 = (f32[1024,16]{0,1:T(8,128)}, f32[1024,16]{0,1:T(8,128)S(1)}, u32[]{:S(2)}) copy-start(f32[1024,16]{0,1:T(8,128)S(1)} %reshape.79) | copy-start | bytes 196612
  49.8 0.7 copy-start.14
  143.5 4.7 %copy-start.18 = (bf16[16,1024]{1,0:T(8,128)(2,1)S(1)}, bf16[16,1024]{1,0:T(8,128)(2,1)}, u32[]{:S(2)}) copy-start(bf16[16,1024]{1,0:T(8,128)(2,1)} %param.17) | copy-start | bytes 98308
  151.2 1.4 copy-start.2
  152.5 4.2 %copy-start.15 = (f32[16,48,16]{1,0,2:T(8,128)S(1)}, f32[16,48,16]{1,0,2:T(8,128)}, u32[]{:S(2)}) copy-start(f32[16,48,16]{1,0,2:T(8,128)} %copy-done.14) | copy-start | bytes 147460
  160.3 3.2 %copy-start.4 = (bf16[16,48,16]{2,0,1:T(8,128)(2,1)S(1)}, bf16[16,48,16]{2,0,1:T(8,128)(2,1)}, u32[]{:S(2)}) copy-start(bf16[16,48,16]{2,0,1:T(8,128)(2,1)} %copy.141) | copy-start | bytes 73732
  160.3 3.2 %copy-start.6 = (f32[1024,16]{0,1:T(8,128)S(1)}, f32[1024,16]{0,1:T(8,128)}, u32[]{:S(2)}) copy-start(f32[1024,16]{0,1:T(8,128)} %copy-done.5) | copy-start | bytes 196612
  160.3 5.5 %copy-start.8 = (bf16[16,48,16]{1,2,0:T(8,128)(2,1)S(1)}, bf16[16,48,16]{1,2,0:T(8,128)(2,1)}, u32[]{:S(2)}) copy-start(bf16[16,48,16]{1,2,0:T(8,128)(2,1)} %fusion.55) | copy-start | bytes 73732
  168.2 2.3 copy-start.17
  168.2 2.5 %copy-start.7 = (f32[1024,16]{0,1:T(8,128)S(1)}, f32[1024,16]{0,1:T(8,128)}, u32[]{:S(2)}) copy-start(f32[1024,16]{0,1:T(8,128)} %copy-done.5) | copy-start | bytes 196612
  170.7 8.5 %copy-start.3 = (f32[48,16,1024]{2,1,0:T(8,128)S(1)}, f32[48,16,1024]{2,1,0:T(8,128)}, u32[]{:S(2)}) copy-start(f32[48,16,1024]{2,1,0:T(8,128)} %get-tuple-element.14) | copy-start | bytes 9437188
  170.7 8.5 %copy-start.11 = (f32[48,1024]{1,0:T(8,128)S(1)}, f32[48,1024]{1,0:T(8,128)}, u32[]{:S(2)}) copy-start(f32[48,1024]{1,0:T(8,128)} %copy-done.10) | copy-start | bytes 589828
  170.7 8.5 %copy-start.13 = (bf16[48,4,16]{2,1,0:T(4,128)(2,1)S(1)}, bf16[48,4,16]{2,1,0:T(4,128)(2,1)}, u32[]{:S(2)}) copy-start(bf16[48,4,16]{2,1,0:T(4,128)(2,1)} %copy-done.12) | copy-start | bytes 18436
  170.7 8.5 %copy-start.21 = (pred[48]{0:T(512)(128)(4,1)S(1)}, pred[48]{0:T(512)(128)(4,1)}, u32[]{:S(2)}) copy-start(pred[48]{0:T(512)(128)(4,1)} %copy-done.20) | copy-start | bytes 148
  182.8 3.5 %copy-start.19 = (pred[8,9]{1,0:T(8,128)(4,1)S(1)}, pred[8,9]{1,0:T(8,128)(4,1)}, u32[]{:S(2)}) copy-start(pred[8,9]{1,0:T(8,128)(4,1)} %broadcast_in_dim.69) | copy-start | bytes 220
  184.8 7.0 %copy-start.9 = (bf16[16,48,16]{1,2,0:T(8,128)(2,1)S(1)}, bf16[16,48,16]{1,2,0:T(8,128)(2,1)}, u32[]{:S(2)}) copy-start(bf16[16,48,16]{1,2,0:T(8,128)(2,1)} %fusion.55) | copy-start | bytes 73732
  187.6 21.6 %all-to-all-start.3 = ((f32[8,32,9,128]{3,1,2,0:T(8,128)}), f32[8,32,9,128]{3,1,2,0:T(8,128)}, u32[]{:S(2)}, u32[]{:S(2)}) async-start(f32[8,32,9,128]{3,1,2,0:T(8,128)} %select_bitcast_fusion), calls=%async_computation.3 | async-start | bytes 2359296 | tf_op jit(solution)/shard_map/all_to_all | solution.py:123
  211.3 18.1 %all-to-all-start.4 = ((f32[32,9,128]{2,1,0:T(8,128)}), f32[32,9,128]{2,1,0:T(8,128)S(1)}, u32[]{:S(2)}, u32[]{:S(2)}) async-start(f32[32,9,128]{2,1,0:T(8,128)} %copy.144), calls=%async_computation.4 | async-start | bytes 524288 | tf_op jit(solution)/shard_map/all_to_all | solution.py:124
